TPU v7x, 512 devices: a whole 4x8x8 slice. The times are simulated.
512 devices in a mesh: wide: 64 (over z, x, core), narrow: 8 (over y).
Axes of the slice: x: 4, y: 8, z: 8, core: 2. Of those that a mesh axis runs over, the one named last changes fastest.
Arguments:
- hidden_in: bfloat16 [16384, 2048], P('wide', 'narrow'), may hold values from -6 to 6
- segment_ids: int32 [16384], P('wide'), may hold values from 0 to 31, never falling along the last dimension, each value on 1 to 2048 neighbouring positions
- page_table: int32 [1024], P('wide'), may hold values from 0 to 1023, as said below
- wq: bfloat16 [2048, 2048], P('wide', 'narrow')
- wk: bfloat16 [2048, 2048], P('wide', 'narrow')
- wv: bfloat16 [2048, 2048], P('wide', 'narrow'), may hold values from -0.125 to 0.125
- wo: bfloat16 [2048, 2048], P('narrow', 'wide'), may hold values from -0.125 to 0.125
- wg: bfloat16 [2048, 4096], P('wide', 'narrow'), may hold values from -0.125 to 0.125
- wu: bfloat16 [2048, 4096], P('wide', 'narrow'), may hold values from -0.125 to 0.125
- wd: bfloat16 [4096, 2048], P('narrow', 'wide'), may hold values from -0.09375 to 0.09375
Outputs:
- result: bfloat16 [16384, 2048], P('wide', 'narrow')
- kv_cache: bfloat16 [2, 1024, 16, 2048], P(None, 'wide', None, 'narrow')
Inputs may be any that keep to these rules, and one draw needn't show every extreme that they name: `page_table`: entries 16 * w to 16 * (w + 1) - 1 of the table are a permutation of those same numbers, for every w.
All inputs are finite; a program needn't handle non-finite values.
Results may differ from a plain program's by a relative error of at most 0.017.
Values may be sent and summed in bfloat16 or wider, within the bound.
No kernel may reach another device: no remote copies, remote signals or barrier semaphores. Data moves between devices by JAX's collectives and lax.ppermute only.
A program may use at most 64 MiB of HBM per device.

v0:
```python
import jax
import jax.numpy as jnp
from jax import lax
from jax.sharding import PartitionSpec as P

HEAD_DIM = 128
REACH = 8
PAGE = 16
epsilon = 1e-05
rope_base = 10000.0


def prefix(value, axis, join, neutral):
    count, mine = (lax.axis_size(axis), lax.axis_index(axis))
    pieces = jax.tree.map(lambda part: lax.all_gather(part, axis), value)
    running = jax.tree.map(
        lambda part, zero: jnp.full_like(part, 0) + jnp.asarray(zero, part.dtype), value, neutral
    )

    def lap(position, running):
        longer = join(running, jax.tree.map(lambda part: part[position], pieces))
        return jax.tree.map(lambda new, old: jnp.where(position < mine, new, old), longer, running)

    return lax.fori_loop(0, count - 1, lap, running)


def shifted(value, axis, steps):
    count = lax.axis_size(axis)
    first, last = (max(0, -steps), min(count, count - steps))
    return lax.ppermute(value, axis, [(source, source + steps) for source in range(first, last)])


def norm_rows(source):
    widened = source.astype(jnp.float32)
    center = widened - jnp.mean(widened, axis=-1, keepdims=True)
    spread = jnp.mean(center * center, axis=-1, keepdims=True)
    return (center * lax.rsqrt(spread + epsilon)).astype(jnp.bfloat16)


def rotate(projected, positions):
    head_size = projected.shape[-1]
    half_dim = head_size // 2
    frequency = jnp.power(rope_base, -jnp.arange(half_dim, dtype=jnp.float32) * 2.0 / head_size)
    angles = positions.astype(jnp.float32)[:, None] * frequency[None, :]
    cosine = jnp.cos(angles)[:, None, :]
    sine_part = jnp.sin(angles)[:, None, :]
    first_half = projected[..., :half_dim]
    second_half = projected[..., half_dim:]
    return jnp.concatenate(
        [
            first_half * cosine - second_half * sine_part,
            second_half * cosine + first_half * sine_part,
        ],
        axis=-1,
    )


def join_runs(earlier, later):
    early_last, early_trailing, early_single = earlier
    late_last, late_trailing, late_single = later
    late_empty = late_trailing == 0
    same_id = (early_last == late_last).astype(jnp.int32)
    linked = (late_single == 1) & (same_id == 1) & (early_trailing > 0)
    last_id = jnp.where(late_empty, early_last, late_last)
    trailing = jnp.where(
        late_empty, early_trailing, late_trailing + jnp.where(linked, early_trailing, 0)
    )
    single = jnp.where(
        late_empty,
        early_single,
        jnp.where(early_trailing == 0, late_single, late_single * early_single * same_id),
    )
    return (last_id, trailing, single)


def add_rows(source, piece):
    return jnp.dot(source, piece, preferred_element_type=jnp.float32)


def per_device(hidden_in, segment_ids, page_table, wq, wk, wv, wo, wg, wu, wd):
    tok_rows = hidden_in.shape[0]
    wide_rank = lax.axis_index("wide")
    local_index = jnp.arange(tok_rows, dtype=jnp.int32)
    run_last = segment_ids[tok_rows - 1]
    run_trailing = jnp.sum((segment_ids == run_last).astype(jnp.int32))
    run_single = (segment_ids[0] == run_last).astype(jnp.int32)
    earlier = prefix(
        (run_last, run_trailing, run_single),
        "wide",
        join_runs,
        (jnp.int32(-1), jnp.int32(0), jnp.int32(1)),
    )
    lower_count = jnp.sum((segment_ids[None, :] < segment_ids[:, None]).astype(jnp.int32), axis=1)
    carried = jnp.where(
        (segment_ids == earlier[0]) & (segment_ids == segment_ids[0]), earlier[1], 0
    )
    positions = local_index - lower_count + carried
    global_index = wide_rank * tok_rows + local_index
    query_start = global_index - positions
    whole = lax.all_gather(hidden_in, "narrow", axis=1, tiled=True)
    normed = norm_rows(whole)
    local_width = wq.shape[1]
    head_count = local_width // HEAD_DIM

    def add_normed(piece):
        return add_rows(normed, piece)

    q_proj = add_normed(lax.all_gather(wq, "wide", axis=0, tiled=True))
    k_proj = add_normed(lax.all_gather(wk, "wide", axis=0, tiled=True))
    v_proj = add_normed(lax.all_gather(wv, "wide", axis=0, tiled=True))
    queries = rotate(q_proj.reshape(tok_rows, head_count, HEAD_DIM), positions).astype(jnp.bfloat16)
    keys_rot = rotate(k_proj.reshape(tok_rows, head_count, HEAD_DIM), positions).astype(
        jnp.bfloat16
    )
    values = v_proj.astype(jnp.bfloat16).reshape(tok_rows, head_count, HEAD_DIM)
    current = (keys_rot, values)
    blocks = [current]
    for step_back in range(REACH):
        current = shifted((current[0], current[1]), "wide", 1)
        blocks.append(current)
    score_scale = HEAD_DIM ** (-0.5)
    ordered = blocks[::-1]
    key_all = jnp.concatenate([member[0] for member in ordered], axis=0)
    value_all = jnp.concatenate([member[1] for member in ordered], axis=0)
    key_index = (wide_rank - REACH) * tok_rows + jnp.arange((REACH + 1) * tok_rows, dtype=jnp.int32)
    allowed = (key_index[None, :] >= query_start[:, None]) & (
        key_index[None, :] <= global_index[:, None]
    )
    scores = (
        jnp.einsum("qhd,khd->hqk", queries, key_all, preferred_element_type=jnp.float32)
        * score_scale
    )
    scores = jnp.where(allowed[None], scores, -1e30)
    row_peak = jnp.max(scores, axis=-1, keepdims=True)
    exps = jnp.where(allowed[None], jnp.exp(scores - row_peak), 0.0)
    attn_probs = (exps / jnp.sum(exps, axis=-1, keepdims=True)).astype(jnp.bfloat16)
    mixed = jnp.einsum("hqk,khd->qhd", attn_probs, value_all, preferred_element_type=jnp.float32)
    attended = mixed.astype(jnp.bfloat16).reshape(tok_rows, local_width)
    attn_terms = jnp.dot(
        attended, lax.all_gather(wo, "wide", axis=1, tiled=True), preferred_element_type=jnp.float32
    )
    attn_sum = lax.psum_scatter(
        attn_terms.astype(jnp.bfloat16), "narrow", scatter_dimension=1, tiled=True
    ).astype(jnp.float32)
    first_res = (hidden_in.astype(jnp.float32) + attn_sum).astype(jnp.bfloat16)
    whole_two = lax.all_gather(first_res, "narrow", axis=1, tiled=True)
    normed_two = norm_rows(whole_two)

    def add_second(piece):
        return add_rows(normed_two, piece)

    gate_proj = add_second(lax.all_gather(wg, "wide", axis=0, tiled=True))
    up_proj = add_second(lax.all_gather(wu, "wide", axis=0, tiled=True))
    hidden = (jax.nn.silu(gate_proj) * up_proj).astype(jnp.bfloat16)
    down_terms = jnp.dot(
        hidden, lax.all_gather(wd, "wide", axis=1, tiled=True), preferred_element_type=jnp.float32
    )
    down_sum = lax.psum_scatter(
        down_terms.astype(jnp.bfloat16), "narrow", scatter_dimension=1, tiled=True
    ).astype(jnp.float32)
    result = (first_res.astype(jnp.float32) + down_sum).astype(jnp.bfloat16)
    page_count = tok_rows // PAGE
    slots = page_table - wide_rank * page_count
    pairs = jnp.stack(
        [
            keys_rot.reshape(page_count, PAGE, local_width),
            values.reshape(page_count, PAGE, local_width),
        ],
        axis=0,
    )
    kv_cache = jnp.zeros_like(pairs).at[:, slots].set(pairs)
    return (result, kv_cache)


def solution(mesh):
    return jax.shard_map(
        per_device,
        mesh=mesh,
        in_specs=(
            P("wide", "narrow"),
            P("wide"),
            P("wide"),
            P("wide", "narrow"),
            P("wide", "narrow"),
            P("wide", "narrow"),
            P("narrow", "wide"),
            P("wide", "narrow"),
            P("wide", "narrow"),
            P("narrow", "wide"),
        ),
        out_specs=(P("wide", "narrow"), P(None, "wide", None, "narrow")),
        check_vma=False,
    )
```

profile of v0, /device:TPU:2, one launch (start us, length us, event | category | flops | bytes accessed | tf_op | source)
XLA Modules:
  0.0 878.4 jit_solution(14633172779645840433)
XLA Ops:
  11.0 1.3 dynamic-slice
  12.3 2.0 fusion.47
  14.3 2.0 fusion.27
  18.3 1.4 dynamic-update-slice
  19.8 25.7 %all-reduce.3 = (s32[64]{0:T(128)S(1)}, s32[64]{0:T(128)S(1)}, s32[64]{0:T(128)S(1)}) all-reduce(s32[64]{0:T(128)S(1)} %dynamic-update-slice, s32[64]{0:T(128)S(1)} %get-tuple-element.159, s32[64]{0:T(128)S(1)} %dynamic-update-slice.2), channel_id=1, replica_groups=mesh['wide'=64,'narrow'=8] {'wide'}, use_global_device_ids=true, to_apply=%add | all-reduce | flops 192 | bytes 1536
  45.5 335.9 %while.15 = (s32[]{:T(128)}, s32[]{:T(128)}, s32[]{:T(128)}, s32[]{:T(128)}, s32[64]{0:T(128)S(1)}, /*index=5*/s32[64]{0:T(128)S(1)}, s32[64]{0:T(128)S(1)}, s32[]{:T(128)}, s32[]{:T(128)}, s32[1]{0:T(128)}) while((s32[]{:T(128)}, s32[]{:T(128)}, s32[]{:T(128)}, s32[]{:T(128)}, s32[64]{0:T(128)S(1)}, /*index=5*/s32[64]{0:T(128)S(1)}, ...), condition=%wide.region_5.6_spmd, body=%wide.region_4.5_spmd.sunk | while | flops 17 | bytes 279 | solution.py:24
  381.3 1.3 fusion.43
  383.2 1.5 convert_reduce_fusion.1
  385.6 1.7 fusion.52
  387.8 1.9 collective-permute-start.8
  389.8 1.7 convolution_convert_fusion.2
  391.6 2.5 collective-permute-start
  394.1 1.9 collective-permute-start.9
  396.1 1.8 collective-permute-done
  397.9 1.9 collective-permute-start.1
  400.4 1.9 collective-permute-start.10
  402.4 1.7 collective-permute-done.1
  404.1 1.9 collective-permute-start.2
  406.7 1.9 collective-permute-start.11
  408.6 1.8 collective-permute-done.2
  410.4 2.2 collective-permute-start.3
  413.1 3.3 collective-permute-start.12
  416.9 4.6 collective-permute-start.4
  421.6 3.6 collective-permute-start.13
  425.2 1.7 fusion.51
  427.0 4.6 collective-permute-start.5
  431.7 3.7 collective-permute-start.14
  435.7 4.7 collective-permute-start.6
  440.4 3.2 collective-permute-start.15
  444.4 5.0 collective-permute-start.7
  452.5 1.4 constant_dynamic-update-slice_fusion.5
  454.0 1.0 copy-done.8
  455.0 5.9 fusion.48
  460.9 3.7 fusion.15
  464.6 22.8 %all-gather.18.cloned.1.call-done = bf16[256,2048]{0,1:T(8,128)(2,1)} async-done(((bf16[256,32]{0,1:T(8,128)(2,1)}), bf16[256,2048]{0,1:T(8,128)(2,1)}) %all-gather.18.cloned.1.call-update) | async-done | bytes 1048592 | tf_op jit(solution)/shard_map/all_gather | solution.py:140
  487.4 2.7 convolution_convert_fusion.1
  490.2 39.1 %reduce-scatter.3.cloned.1.call-done = bf16[256,256]{1,0:T(8,128)(2,1)} async-done(((bf16[256,2048]{1,0:T(8,128)(2,1)}), bf16[256,256]{1,0:T(8,128)(2,1)}) %reduce-scatter.3.cloned.1.call-update) | async-done | bytes 131088 | tf_op jit(solution)/shard_map/reduce_scatter | solution.py:142
  529.3 1.6 add_convert_fusion.1
  533.2 40.0 %all-gather.20.cloned.1.call-done = bf16[256,2048]{1,0:T(8,128)(2,1)} async-done(((bf16[256,256]{1,0:T(8,128)(2,1)}), bf16[256,2048]{1,0:T(8,128)(2,1)}) %all-gather.20.cloned.1.call-update) | async-done | bytes 1048592 | tf_op jit(solution)/shard_map/all_gather | solution.py:146
  573.2 1.5 convert_reduce_fusion
  575.2 83.4 %all-gather.22.cloned.1.call-done = bf16[2048,512]{1,0:T(8,128)(2,1)} async-done(((bf16[32,512]{1,0:T(8,128)(2,1)}), bf16[2048,512]{1,0:T(8,128)(2,1)}) %all-gather.22.cloned.1.call-update) | async-done | bytes 2097168 | tf_op jit(solution)/shard_map/all_gather | solution.py:152
  658.6 2.3 fusion.41
  660.9 81.6 %all-gather.24.cloned.1.call-done = bf16[2048,512]{1,0:T(8,128)(2,1)} async-done(((bf16[32,512]{1,0:T(8,128)(2,1)}), bf16[2048,512]{1,0:T(8,128)(2,1)}) %all-gather.24.cloned.1.call-update) | async-done | bytes 2097168 | tf_op jit(solution)/shard_map/all_gather | solution.py:153
  742.6 83.8 %all-gather.26.cloned.1.call-done = bf16[512,2048]{0,1:T(8,128)(2,1)} async-done(((bf16[512,32]{0,1:T(8,128)(2,1)}), bf16[512,2048]{0,1:T(8,128)(2,1)}) %all-gather.26.cloned.1.call-update) | async-done | bytes 2097168 | tf_op jit(solution)/shard_map/all_gather | solution.py:156
  826.4 4.7 convolution_convert_fusion
  831.5 1.2 scatter_fusion
  832.7 37.6 %reduce-scatter.5.cloned.1.call-done = bf16[256,256]{1,0:T(8,128)(2,1)} async-done(((bf16[256,2048]{1,0:T(8,128)(2,1)}), bf16[256,256]{1,0:T(8,128)(2,1)}) %reduce-scatter.5.cloned.1.call-update) | async-done | bytes 131088 | tf_op jit(solution)/shard_map/reduce_scatter | solution.py:158
  870.3 1.6 add_convert_fusion
  (297 shorter events, 139.8 us)
Async XLA Ops:
  7.2 376.1 %all-gather.10.cloned.1.call-start = ((), (), s32[]{:S(2)}) async-start(), calls=%async_computation.2 | async-start | bytes 1179648 | tf_op jit(solution)/shard_map/all_gather | solution.py:100
  7.9 377.7 %all-gather.16.cloned.1.call-start = ((), (), s32[]{:S(2)}) async-start(), calls=%async_computation.5 | async-start | bytes 1064960 | tf_op jit(solution)/shard_map/all_gather | solution.py:109
  8.6 381.1 %all-gather.12.cloned.1.call-start = ((), (), s32[]{:S(2)}) async-start(), calls=%async_computation.3 | async-start | bytes 1064960 | tf_op jit(solution)/shard_map/all_gather | solution.py:110
  9.4 415.9 %all-gather.14.cloned.1.call-start = ((), (), s32[]{:S(2)}) async-start(), calls=%async_computation.4 | async-start | bytes 1064960 | tf_op jit(solution)/shard_map/all_gather | solution.py:108
  10.0 477.4 %all-gather.18.cloned.1.call-start = ((), (), s32[]{:S(2)}) async-start(), calls=%async_computation.6 | async-start | bytes 1064960 | tf_op jit(solution)/shard_map/all_gather | solution.py:140
  383.2 1.6 copy-start
  387.8 6.3 collective-permute-start.8
  391.6 6.3 collective-permute-start
  394.1 6.3 collective-permute-start.9
  397.9 6.3 collective-permute-start.1
  400.4 6.3 collective-permute-start.10
  402.4 126.9 %reduce-scatter.3.cloned.1.call-start = ((), (), s32[]{:S(2)}) async-start(), calls=%async_computation.7 | async-start | bytes 1179648 | tf_op jit(solution)/shard_map/reduce_scatter | solution.py:142
  404.1 6.3 collective-permute-start.2
  406.7 6.4 collective-permute-start.11
  410.4 6.5 collective-permute-start.3
  413.1 8.5 collective-permute-start.12
  416.9 10.1 %collective-permute-start.4 = (bf16[256,2,128]{0,2,1:T(8,128)(2,1)S(1)}, bf16[256,2,128]{0,2,1:T(8,128)(2,1)}, u32[]{:S(2)}, u32[]{:S(2)}) collective-permute-start(bf16[256,2,128]{0,2,1:T(8,128)(2,1)S(1)} %collective-permute-done.3), channel_id=1, source_target_pairs={{0,8},{8,16},{16,24},{24,32},{32,40},{40,48},{48,56},{56,64},{64,7... | collective-permute-start | bytes 393224 | tf_op jit(solution)/shard_map/ppermute | solution.py:30
  421.6 10.1 %collective-permute-start.13 = (bf16[256,2,128]{2,0,1:T(8,128)(2,1)}, bf16[256,2,128]{2,0,1:T(8,128)(2,1)}, u32[]{:S(2)}, u32[]{:S(2)}) collective-permute-start(bf16[256,2,128]{2,0,1:T(8,128)(2,1)} %collective-permute-done.12), channel_id=1, source_target_pairs={{0,8},{8,16},{16,24},{24,32},{32,40},{40,48},{48,56},{56,64},{64,7... | collective-permute-start | bytes 393224 | tf_op jit(solution)/shard_map/ppermute | solution.py:30
  427.0 8.6 collective-permute-start.5
  431.7 8.7 collective-permute-start.14
  435.7 8.7 collective-permute-start.6
  440.4 8.9 %collective-permute-start.15 = (bf16[256,2,128]{2,0,1:T(8,128)(2,1)S(1)}, bf16[256,2,128]{2,0,1:T(8,128)(2,1)S(1)}, u32[]{:S(2)}, u32[]{:S(2)}) collective-permute-start(bf16[256,2,128]{2,0,1:T(8,128)(2,1)S(1)} %collective-permute-done.14), channel_id=1, source_target_pairs={{0,8},{8,16},{16,24},{24,32},{32,40},{40,48},{48,56},{56,64},{64,7... | collective-permute-start | bytes 393224 | tf_op jit(solution)/shard_map/ppermute | solution.py:30
  444.4 8.1 collective-permute-start.7
  452.4 1.6 copy-start.7
  452.4 2.6 copy-start.5
  452.4 2.6 copy-start.6
  454.0 1.0 copy-start.8
  487.4 41.9 %copy-start.4 = (bf16[256,256]{1,0:T(8,128)(2,1)S(1)}, bf16[256,256]{1,0:T(8,128)(2,1)}, u32[]{:S(2)}) copy-start(bf16[256,256]{1,0:T(8,128)(2,1)} %param.12) | copy-start | bytes 393220
  490.1 83.1 %all-gather.20.cloned.1.call-start = ((), (), s32[]{:S(2)}) async-start(), calls=%async_computation.8 | async-start | bytes 1179648 | tf_op jit(solution)/shard_map/all_gather | solution.py:146
  530.9 127.7 %all-gather.22.cloned.1.call-start = ((), (), s32[]{:S(2)}) async-start(), calls=%async_computation.9 | async-start | bytes 2129920 | tf_op jit(solution)/shard_map/all_gather | solution.py:152
  531.7 210.9 %all-gather.24.cloned.1.call-start = ((), (), s32[]{:S(2)}) async-start(), calls=%async_computation.10 | async-start | bytes 2129920 | tf_op jit(solution)/shard_map/all_gather | solution.py:153
  532.4 294.0 %all-gather.26.cloned.1.call-start = ((), (), s32[]{:S(2)}) async-start(), calls=%async_computation.11 | async-start | bytes 2129920 | tf_op jit(solution)/shard_map/all_gather | solution.py:156
  533.0 337.3 %reduce-scatter.5.cloned.1.call-start = ((), (), s32[]{:S(2)}) async-start(), calls=%async_computation.12 | async-start | bytes 1179648 | tf_op jit(solution)/shard_map/reduce_scatter | solution.py:158
  573.2 1.5 copy-start.1
  660.9 170.2 %copy-start.9 = (s32[16]{0:T(128)S(1)}, s32[16]{0:T(128)}, u32[]{:S(2)}) copy-start(s32[16]{0:T(128)} %param.14) | copy-start | bytes 196
  831.3 39.0 %copy-start.2 = (bf16[256,256]{1,0:T(8,128)(2,1)S(1)}, bf16[256,256]{1,0:T(8,128)(2,1)}, u32[]{:S(2)}) copy-start(bf16[256,256]{1,0:T(8,128)(2,1)} %add_convert_fusion.1) | copy-start | bytes 393220
  832.7 39.2 %copy-start.3 = (bf16[2,16,16,256]{3,2,1,0:T(8,128)(2,1)}, bf16[2,16,16,256]{3,2,1,0:T(8,128)(2,1)S(1)}, u32[]{:S(2)}) copy-start(bf16[2,16,16,256]{3,2,1,0:T(8,128)(2,1)S(1)} %scatter_fusion) | copy-start | bytes 786436
Sparse Core Ops, SparseCore 0:
  10.0 46.6 all-gather.9
  60.1 81.1 all-gather.15
  144.6 79.8 all-gather.11
  227.7 79.7 all-gather.13
  402.5 84.8 all-gather.17
  490.2 38.9 reduce-scatter.2
  531.9 41.2 all-gather.19
  576.6 81.9 all-gather.21
  661.9 80.5 all-gather.23
  745.8 80.5 all-gather.25
  831.2 39.0 reduce-scatter.4
where the time goes:
time: 882 us; the launch traced here: 878 us
  waiting for transfers between devices  400 us (45%)
  loops' own time  212 us (24%)
  local copies, waits for them, and re-layouts  137 us (16%)
  starting transfers between devices  49.6 us (6%)
  blocking collectives  25.7 us (3%)
  matrix products  24.5 us (3%)
  between operations  15.8 us (2%)
  other arithmetic  13.9 us (2%)
    another operation x1, loops' own time, prefix(): return lax.fori_loop(0, count - 1, lap, running)  212 us
    dynamic_slice x189, local copies, waits for them, and re-layouts, lap(): longer = join(running, jax.tree.map(lambda part: part[position], pieces))  124 us
    all_gather x1, waiting for transfers between devices, per_device(): lax.all_gather(wd, 'wide', axis=1, tiled=True)  83.8 us
    all_gather x1, waiting for transfers between devices, per_device(): gate_proj = add_second(lax.all_gather(wg, 'wide', axis=0, tiled=True))  83.4 us
    all_gather x1, waiting for transfers between devices, per_device(): up_proj = add_second(lax.all_gather(wu, 'wide', axis=0, tiled=True))  81.6 us
    ppermute x16, starting transfers between devices, shifted(): lax.ppermute(value, axis, [(source, source + steps) for source in range(f...  49 us
    all_gather x1, waiting for transfers between devices, per_device(): whole_two = lax.all_gather(first_res, 'narrow', axis=1, tiled=True)  40 us
    reduce_scatter x1, waiting for transfers between devices, per_device(): lax.psum_scatter(attn_terms.astype(jnp.bfloat16), 'narrow', scatter_dimen...  39.1 us
  transfers between devices with their start and end apart: 27, of which 13 were waited for; matrix products, arithmetic and copies ran while one was open for 19% of the time, Pallas kernels for 0%

commit v1 on v0

--- a/solution.py
+++ b/solution.py
@@ -8,6 +8,28 @@
 PAGE = 16
 epsilon = 1e-05
 rope_base = 10000.0
+
+
+def joined_along(blocks, dim):
+    shape = list(blocks.shape[1:])
+    shape[dim] *= blocks.shape[0]
+    return jnp.moveaxis(blocks, 0, dim).reshape(shape)
+
+
+def gather_around(shard, axis, dim):
+    size = lax.axis_size(axis)
+    pairs = [(i, (i + 1) % size) for i in range(size)]
+    back = [(b, a) for a, b in pairs]
+    lower, upper = ([], [])
+    for step in range(size - 1):
+        if step % 2 == 0:
+            lower.append(lax.ppermute(lower[-1] if lower else shard, axis, pairs))
+        else:
+            upper.append(lax.ppermute(upper[-1] if upper else shard, axis, back))
+    parts = jnp.stack([*lower[::-1], shard, *upper])
+    shift = lax.axis_index(axis) - len(lower)
+    parts = parts[(jnp.arange(size) - shift) % size]
+    return joined_along(parts, dim)
 
 
 def prefix(value, axis, join, neutral):
@@ -143,7 +165,7 @@
         attn_terms.astype(jnp.bfloat16), "narrow", scatter_dimension=1, tiled=True
     ).astype(jnp.float32)
     first_res = (hidden_in.astype(jnp.float32) + attn_sum).astype(jnp.bfloat16)
-    whole_two = lax.all_gather(first_res, "narrow", axis=1, tiled=True)
+    whole_two = gather_around(first_res, "narrow", 1)
     normed_two = norm_rows(whole_two)
 
     def add_second(piece):

time: 882 us -> 820 us (0.930)
  the two profiles are of different devices: /device:TPU:2 before, /device:TPU:4 now
where the time goes in v1:
time: 820 us; the launch traced here: 815 us
  waiting for transfers between devices  323 us (39%)
  loops' own time  200 us (24%)
  local copies, waits for them, and re-layouts  132 us (16%)
  starting transfers between devices  81.7 us (10%)
  blocking collectives  24.7 us (3%)
  matrix products  24.1 us (3%)
  between operations  16.3 us (2%)
  other arithmetic  13.8 us (2%)
    another operation x1, loops' own time, prefix(): return lax.fori_loop(0, count - 1, lap, running)  200 us
    dynamic_slice x189, local copies, waits for them, and re-layouts, lap(): longer = join(running, jax.tree.map(lambda part: part[position], pieces))  117 us
    all_gather x1, waiting for transfers between devices, per_device(): lax.all_gather(wd, 'wide', axis=1, tiled=True)  84 us
    all_gather x1, waiting for transfers between devices, per_device(): up_proj = add_second(lax.all_gather(wu, 'wide', axis=0, tiled=True))  81.6 us
    ppermute x16, starting transfers between devices, shifted(): lax.ppermute(value, axis, [(source, source + steps) for source in range(f...  56.8 us
    all_gather x1, waiting for transfers between devices, per_device(): gate_proj = add_second(lax.all_gather(wg, 'wide', axis=0, tiled=True))  43.5 us
    reduce_scatter x1, waiting for transfers between devices, per_device(): lax.psum_scatter(attn_terms.astype(jnp.bfloat16), 'narrow', scatter_dimen...  37.8 us
    reduce_scatter x1, waiting for transfers between devices, per_device(): lax.psum_scatter(down_terms.astype(jnp.bfloat16), 'narrow', scatter_dimen...  37.7 us
  transfers between devices with their start and end apart: 33, of which 13 were waited for; matrix products, arithmetic and copies ran while one was open for 20% of the time, Pallas kernels for 0%

profile of v1, /device:TPU:4, one launch (start us, length us, event | category | flops | bytes accessed | tf_op | source)
XLA Modules:
  0.0 815.2 jit_solution(16800686309239877116)
XLA Ops:
  12.2 1.9 fusion.45
  14.1 2.0 fusion.27
  19.4 24.7 %all-reduce.3 = (s32[64]{0:T(128)S(1)}, s32[64]{0:T(128)S(1)}, s32[64]{0:T(128)S(1)}) all-reduce(s32[64]{0:T(128)S(1)} %dynamic-update-slice, s32[64]{0:T(128)S(1)} %get-tuple-element.159, s32[64]{0:T(128)S(1)} %dynamic-update-slice.2), channel_id=1, replica_groups=mesh['wide'=64,'narrow'=8] {'wide'}, use_global_device_ids=true, to_apply=%add | all-reduce | flops 192 | bytes 1536
  44.1 316.6 %while.15 = (s32[]{:T(128)}, s32[]{:T(128)}, s32[]{:T(128)}, s32[]{:T(128)}, s32[64]{0:T(128)S(1)}, /*index=5*/s32[64]{0:T(128)S(1)}, s32[64]{0:T(128)S(1)}, s32[]{:T(128)}, s32[]{:T(128)}, s32[1]{0:T(128)}) while((s32[]{:T(128)}, s32[]{:T(128)}, s32[]{:T(128)}, s32[]{:T(128)}, s32[64]{0:T(128)S(1)}, /*index=5*/s32[64]{0:T(128)S(1)}, ...), condition=%wide.region_5.6_spmd, body=%wide.region_4.5_spmd.sunk | while | flops 17 | bytes 279 | solution.py:46
  362.7 1.5 convert_reduce_fusion.1
  365.0 1.7 fusion.50
  367.3 1.9 collective-permute-start.8
  369.2 1.7 convolution_convert_fusion.2
  371.0 3.5 collective-permute-start
  374.5 1.9 collective-permute-start.9
  377.3 3.6 collective-permute-start.1
  380.9 1.9 collective-permute-start.10
  383.6 4.0 collective-permute-start.2
  387.5 3.7 collective-permute-start.11
  391.3 4.6 collective-permute-start.3
  396.0 3.6 collective-permute-start.12
  400.2 4.6 collective-permute-start.4
  404.8 3.7 collective-permute-start.13
  408.5 1.7 fusion.49
  410.3 4.7 collective-permute-start.5
  415.1 3.1 collective-permute-start.14
  418.5 5.0 collective-permute-start.6
  423.6 1.9 collective-permute-start.15
  426.3 5.0 collective-permute-start.7
  436.9 6.0 fusion.46
  442.9 3.3 fusion.15
  446.2 21.5 %all-gather.17.cloned.1.call-done = bf16[256,2048]{0,1:T(8,128)(2,1)} async-done(((bf16[256,32]{0,1:T(8,128)(2,1)}), bf16[256,2048]{0,1:T(8,128)(2,1)}) %all-gather.17.cloned.1.call-update) | async-done | bytes 1048592 | tf_op jit(solution)/shard_map/all_gather | solution.py:162
  467.7 2.8 convolution_convert_fusion.1
  472.0 37.8 %reduce-scatter.3.cloned.1.call-done = bf16[256,256]{1,0:T(8,128)(2,1)} async-done(((bf16[256,2048]{1,0:T(8,128)(2,1)}), bf16[256,256]{1,0:T(8,128)(2,1)}) %reduce-scatter.3.cloned.1.call-update) | async-done | bytes 131088 | tf_op jit(solution)/shard_map/reduce_scatter | solution.py:164
  510.8 2.9 collective-permute-start.16
  513.7 5.2 collective-permute-done.16
  518.8 2.4 collective-permute-start.17
  521.3 4.6 collective-permute-start.20
  525.9 2.1 collective-permute-done.17
  528.0 1.9 collective-permute-start.18
  530.1 5.2 collective-permute-start.21
  536.7 1.9 collective-permute-start.19
  538.6 5.5 collective-permute-start.22
  544.8 1.6 collective-permute-done.22
  547.0 1.6 convert_bitcast_fusion
  548.6 1.9 copy.34
  551.4 43.5 %all-gather.19.cloned.1.call-done = bf16[2048,512]{1,0:T(8,128)(2,1)} async-done(((bf16[32,512]{1,0:T(8,128)(2,1)}), bf16[2048,512]{1,0:T(8,128)(2,1)}) %all-gather.19.cloned.1.call-update) | async-done | bytes 2097168 | tf_op jit(solution)/shard_map/all_gather | solution.py:174
  594.9 2.3 fusion.51
  597.2 81.6 %all-gather.21.cloned.1.call-done = bf16[2048,512]{1,0:T(8,128)(2,1)} async-done(((bf16[32,512]{1,0:T(8,128)(2,1)}), bf16[2048,512]{1,0:T(8,128)(2,1)}) %all-gather.21.cloned.1.call-update) | async-done | bytes 2097168 | tf_op jit(solution)/shard_map/all_gather | solution.py:175
  678.9 84.0 %all-gather.23.cloned.1.call-done = bf16[512,2048]{0,1:T(8,128)(2,1)} async-done(((bf16[512,32]{0,1:T(8,128)(2,1)}), bf16[512,2048]{0,1:T(8,128)(2,1)}) %all-gather.23.cloned.1.call-update) | async-done | bytes 2097168 | tf_op jit(solution)/shard_map/all_gather | solution.py:178
  762.9 4.6 convolution_convert_fusion
  769.1 37.7 %reduce-scatter.5.cloned.1.call-done = bf16[256,256]{1,0:T(8,128)(2,1)} async-done(((bf16[256,2048]{1,0:T(8,128)(2,1)}), bf16[256,256]{1,0:T(8,128)(2,1)}) %reduce-scatter.5.cloned.1.call-update) | async-done | bytes 131088 | tf_op jit(solution)/shard_map/reduce_scatter | solution.py:180
  806.7 1.6 add_convert_fusion
  (320 shorter events, 143.7 us)
Async XLA Ops:
  7.2 355.5 %all-gather.9.cloned.1.call-start = ((), (), s32[]{:S(2)}) async-start(), calls=%async_computation.2 | async-start | bytes 1179648 | tf_op jit(solution)/shard_map/all_gather | solution.py:122
  7.9 357.1 %all-gather.15.cloned.1.call-start = ((), (), s32[]{:S(2)}) async-start(), calls=%async_computation.5 | async-start | bytes 1064960 | tf_op jit(solution)/shard_map/all_gather | solution.py:131
  8.6 360.6 %all-gather.11.cloned.1.call-start = ((), (), s32[]{:S(2)}) async-start(), calls=%async_computation.3 | async-start | bytes 1064960 | tf_op jit(solution)/shard_map/all_gather | solution.py:132
  9.4 399.1 %all-gather.13.cloned.1.call-start = ((), (), s32[]{:S(2)}) async-start(), calls=%async_computation.4 | async-start | bytes 1064960 | tf_op jit(solution)/shard_map/all_gather | solution.py:130
  10.0 457.7 %all-gather.17.cloned.1.call-start = ((), (), s32[]{:S(2)}) async-start(), calls=%async_computation.6 | async-start | bytes 1064960 | tf_op jit(solution)/shard_map/all_gather | solution.py:162
  362.7 1.6 copy-start
  367.3 7.2 collective-permute-start.8
  371.0 6.3 collective-permute-start
  374.5 6.4 collective-permute-start.9
  377.3 6.3 collective-permute-start.1
  380.9 6.7 collective-permute-start.10
  382.8 127.0 %reduce-scatter.3.cloned.1.call-start = ((), (), s32[]{:S(2)}) async-start(), calls=%async_computation.7 | async-start | bytes 1179648 | tf_op jit(solution)/shard_map/reduce_scatter | solution.py:164
  383.6 7.7 collective-permute-start.2
  387.5 8.4 %collective-permute-start.11 = (bf16[256,2,128]{2,0,1:T(8,128)(2,1)S(1)}, bf16[256,2,128]{2,0,1:T(8,128)(2,1)}, u32[]{:S(2)}, u32[]{:S(2)}) collective-permute-start(bf16[256,2,128]{2,0,1:T(8,128)(2,1)S(1)} %collective-permute-done.10), channel_id=1, source_target_pairs={{0,8},{8,16},{16,24},{24,32},{32,40},{40,48},{48,56},{56,64},{64,7... | collective-permute-start | bytes 393224 | tf_op jit(solution)/shard_map/ppermute | solution.py:52
  391.3 8.8 %collective-permute-start.3 = (bf16[256,2,128]{0,2,1:T(8,128)(2,1)S(1)}, bf16[256,2,128]{0,2,1:T(8,128)(2,1)S(1)}, u32[]{:S(2)}, u32[]{:S(2)}) collective-permute-start(bf16[256,2,128]{0,2,1:T(8,128)(2,1)S(1)} %collective-permute-done.2), channel_id=1, source_target_pairs={{0,8},{8,16},{16,24},{24,32},{32,40},{40,48},{48,56},{56,64},{64,7... | collective-permute-start | bytes 393224 | tf_op jit(solution)/shard_map/ppermute | solution.py:52
  396.0 8.9 %collective-permute-start.12 = (bf16[256,2,128]{2,0,1:T(8,128)(2,1)}, bf16[256,2,128]{2,0,1:T(8,128)(2,1)}, u32[]{:S(2)}, u32[]{:S(2)}) collective-permute-start(bf16[256,2,128]{2,0,1:T(8,128)(2,1)} %collective-permute-done.11), channel_id=1, source_target_pairs={{0,8},{8,16},{16,24},{24,32},{32,40},{40,48},{48,56},{56,64},{64,7... | collective-permute-start | bytes 393224 | tf_op jit(solution)/shard_map/ppermute | solution.py:52
  400.2 10.1 %collective-permute-start.4 = (bf16[256,2,128]{0,2,1:T(8,128)(2,1)S(1)}, bf16[256,2,128]{0,2,1:T(8,128)(2,1)}, u32[]{:S(2)}, u32[]{:S(2)}) collective-permute-start(bf16[256,2,128]{0,2,1:T(8,128)(2,1)S(1)} %collective-permute-done.3), channel_id=1, source_target_pairs={{0,8},{8,16},{16,24},{24,32},{32,40},{40,48},{48,56},{56,64},{64,7... | collective-permute-start | bytes 393224 | tf_op jit(solution)/shard_map/ppermute | solution.py:52
  404.8 10.2 %collective-permute-start.13 = (bf16[256,2,128]{2,0,1:T(8,128)(2,1)}, bf16[256,2,128]{2,0,1:T(8,128)(2,1)}, u32[]{:S(2)}, u32[]{:S(2)}) collective-permute-start(bf16[256,2,128]{2,0,1:T(8,128)(2,1)} %collective-permute-done.12), channel_id=1, source_target_pairs={{0,8},{8,16},{16,24},{24,32},{32,40},{40,48},{48,56},{56,64},{64,7... | collective-permute-start | bytes 393224 | tf_op jit(solution)/shard_map/ppermute | solution.py:52
  410.3 8.2 %collective-permute-start.5 = (bf16[256,2,128]{0,2,1:T(8,128)(2,1)}, bf16[256,2,128]{0,2,1:T(8,128)(2,1)S(1)}, u32[]{:S(2)}, u32[]{:S(2)}) collective-permute-start(bf16[256,2,128]{0,2,1:T(8,128)(2,1)} %collective-permute-done.4), channel_id=1, source_target_pairs={{0,8},{8,16},{16,24},{24,32},{32,40},{40,48},{48,56},{56,64},{64,7... | collective-permute-start | bytes 393224 | tf_op jit(solution)/shard_map/ppermute | solution.py:52
  415.1 8.5 %collective-permute-start.14 = (bf16[256,2,128]{2,0,1:T(8,128)(2,1)}, bf16[256,2,128]{2,0,1:T(8,128)(2,1)S(1)}, u32[]{:S(2)}, u32[]{:S(2)}) collective-permute-start(bf16[256,2,128]{2,0,1:T(8,128)(2,1)} %collective-permute-done.13), channel_id=1, source_target_pairs={{0,8},{8,16},{16,24},{24,32},{32,40},{40,48},{48,56},{56,64},{64,7... | collective-permute-start | bytes 393224 | tf_op jit(solution)/shard_map/ppermute | solution.py:52
  418.5 7.7 collective-permute-start.6
  423.6 7.7 collective-permute-start.15
  426.3 8.1 collective-permute-start.7
  434.3 1.6 copy-start.5
  434.3 2.6 copy-start.3
  434.3 2.6 copy-start.4
  435.9 1.0 copy-start.6
  436.9 6.0 copy-start.7
  467.7 42.1 %copy-start.2 = (bf16[256,256]{1,0:T(8,128)(2,1)S(1)}, bf16[256,256]{1,0:T(8,128)(2,1)}, u32[]{:S(2)}) copy-start(bf16[256,256]{1,0:T(8,128)(2,1)} %param.12) | copy-start | bytes 393220
  470.5 124.4 %all-gather.19.cloned.1.call-start = ((), (), s32[]{:S(2)}) async-start(), calls=%async_computation.8 | async-start | bytes 2129920 | tf_op jit(solution)/shard_map/all_gather | solution.py:174
  471.2 207.6 %all-gather.21.cloned.1.call-start = ((), (), s32[]{:S(2)}) async-start(), calls=%async_computation.9 | async-start | bytes 2129920 | tf_op jit(solution)/shard_map/all_gather | solution.py:175
  472.0 290.9 %all-gather.23.cloned.1.call-start = ((), (), s32[]{:S(2)}) async-start(), calls=%async_computation.10 | async-start | bytes 2129920 | tf_op jit(solution)/shard_map/all_gather | solution.py:178
  510.8 8.1 collective-permute-start.16
  518.8 9.2 %collective-permute-start.17 = (bf16[256,256]{1,0:T(8,128)(2,1)S(1)}, bf16[256,256]{1,0:T(8,128)(2,1)S(1)}, u32[]{:S(2)}, u32[]{:S(2)}) collective-permute-start(bf16[256,256]{1,0:T(8,128)(2,1)S(1)} %collective-permute-done.16), channel_id=1, source_target_pairs={{0,1},{1,2},{2,3},{3,4},{4,5},{5,6},{6,7},{7,0},{8,9},{9,10},{10,1... | collective-permute-start | bytes 393224 | tf_op jit(solution)/shard_map/ppermute | solution.py:26
  521.3 8.8 %collective-permute-start.20 = (bf16[256,256]{1,0:T(8,128)(2,1)S(1)}, bf16[256,256]{1,0:T(8,128)(2,1)S(1)}, u32[]{:S(2)}, u32[]{:S(2)}) collective-permute-start(bf16[256,256]{1,0:T(8,128)(2,1)S(1)} %add_convert_fusion.1), channel_id=1, source_target_pairs={{1,0},{2,1},{3,2},{4,3},{5,4},{6,5},{7,6},{0,7},{9,8},{10,9},{11,1... | collective-permute-start | bytes 393224 | tf_op jit(solution)/shard_map/ppermute | solution.py:28
  528.0 8.6 %collective-permute-start.18 = (bf16[256,256]{1,0:T(8,128)(2,1)S(1)}, bf16[256,256]{1,0:T(8,128)(2,1)S(1)}, u32[]{:S(2)}, u32[]{:S(2)}) collective-permute-start(bf16[256,256]{1,0:T(8,128)(2,1)S(1)} %collective-permute-done.17), channel_id=1, source_target_pairs={{0,1},{1,2},{2,3},{3,4},{4,5},{5,6},{6,7},{7,0},{8,9},{9,10},{10,1... | collective-permute-start | bytes 393224 | tf_op jit(solution)/shard_map/ppermute | solution.py:26
  530.0 276.7 %reduce-scatter.5.cloned.1.call-start = ((), (), s32[]{:S(2)}) async-start(), calls=%async_computation.11 | async-start | bytes 1179648 | tf_op jit(solution)/shard_map/reduce_scatter | solution.py:180
  530.1 8.6 %collective-permute-start.21 = (bf16[256,256]{1,0:T(8,128)(2,1)S(1)}, bf16[256,256]{1,0:T(8,128)(2,1)S(1)}, u32[]{:S(2)}, u32[]{:S(2)}) collective-permute-start(bf16[256,256]{1,0:T(8,128)(2,1)S(1)} %collective-permute-done.20), channel_id=1, source_target_pairs={{1,0},{2,1},{3,2},{4,3},{5,4},{6,5},{7,6},{0,7},{9,8},{10,9},{11,1... | collective-permute-start | bytes 393224 | tf_op jit(solution)/shard_map/ppermute | solution.py:28
  536.7 8.1 collective-permute-start.19
  538.6 7.8 collective-permute-start.22
  597.2 170.3 %copy-start.8 = (s32[16]{0:T(128)S(1)}, s32[16]{0:T(128)}, u32[]{:S(2)}) copy-start(s32[16]{0:T(128)} %param.14) | copy-start | bytes 196
  769.1 39.3 %copy-start.1 = (bf16[2,16,16,256]{3,2,1,0:T(8,128)(2,1)}, bf16[2,16,16,256]{3,2,1,0:T(8,128)(2,1)S(1)}, u32[]{:S(2)}) copy-start(bf16[2,16,16,256]{3,2,1,0:T(8,128)(2,1)S(1)} %scatter_fusion) | copy-start | bytes 786436
Sparse Core Ops, SparseCore 0:
  10.0 46.5 all-gather.8
  60.0 81.2 all-gather.14
  144.6 79.7 all-gather.10
  227.6 79.7 all-gather.12
  382.9 84.7 all-gather.16
  470.6 39.1 reduce-scatter.2
  513.2 81.6 all-gather.18
  598.3 80.5 all-gather.20
  682.2 80.5 all-gather.22
  767.6 39.0 reduce-scatter.4
